TPU v7x, 128 devices: a whole 4x4x4 slice. The times are simulated.
128 devices in a mesh: guid: 2 (over x_hi), req: 4 (over x_lo, core), seq: 16 (over y, z).
Axes of the slice: x: 4 (x_hi: 2, x_lo: 2; x = x_hi * 2 + x_lo), y: 4, z: 4, core: 2. Of those that a mesh axis runs over, the one named last changes fastest.
Arguments:
- img_hidden: bfloat16 [2, 24, 1024, 1536], P('guid', 'req', 'seq'), may hold values from -6 to 6
- txt_hidden: bfloat16 [2, 24, 192, 1536], P('guid', 'req', 'seq'), may hold values from -6 to 6
- img_mod: float32 [2, 24, 5, 1536], P('guid', 'req')
- txt_mod: float32 [2, 24, 2, 1536], P('guid', 'req'), may hold values from -3 to 3
- w_img_qkv: bfloat16 [1536, 3072], P(('guid', 'req', 'seq')), may hold values from -0.15625 to 0.15625
- w_txt_qkv: bfloat16 [1536, 3072], P(('guid', 'req', 'seq')), may hold values from -0.15625 to 0.15625
- w_out: bfloat16 [1024, 1536], P(('guid', 'req', 'seq')), may hold values from -0.1875 to 0.1875
- w_head: bfloat16 [1536, 64], P(('guid', 'req', 'seq')), may hold values from -0.15625 to 0.15625
- text_lengths: int32 [2, 24], P('guid', 'req'), may hold values from 1 to 154, as said below
- latent: float32 [24, 1024, 64], P('req', 'seq', 'guid'), may hold values from -6 to 6
- step: int32 [1], replicated, may hold values from 0 to 27
Outputs:
- advanced: float32 [24, 1024, 64], P('req', 'seq', 'guid')
- guided: float32 [24, 1024, 64], P('req', 'seq', 'guid')
Inputs may be any that keep to these rules, and one draw needn't show every extreme that they name: `text_lengths`: in each half one prompt has 154 text tokens and another has 1.
All inputs are finite; a program needn't handle non-finite values.
Results may differ from a plain program's by a relative error of at most 0.012.
The roundings to bfloat16 on the way count: a program that leaves them out, or rounds other values in their place, can miss the bound.
Values may be sent and summed in bfloat16 or wider, within the bound.
No kernel may reach another device: no remote copies, remote signals or barrier semaphores. Data moves between devices by JAX's collectives and lax.ppermute only.
A program may use at most 192 MiB of HBM per device.

v0:
```python
import jax
import jax.numpy as jnp
from jax import lax
from jax.sharding import PartitionSpec as P

HD = 64
STEPS = 28
norm_epsilon = 1e-06
flow_shift = 3.0
guide_scale = 4.5


def partner(value, axis, bit):
    mask = 2**bit
    pairs = [(source, source ^ mask) for source in range(lax.axis_size(axis))]
    return lax.ppermute(value, axis, pairs)


def modulate(values_in, shift_vec, scale_vec):
    values_in = values_in.astype(jnp.float32)
    average = jnp.mean(values_in, axis=-1, keepdims=True)
    variance = jnp.mean((values_in - average) ** 2, axis=-1, keepdims=True)
    normed = (values_in - average) * lax.rsqrt(variance + norm_epsilon)
    return (normed * (1.0 + scale_vec[..., None, :]) + shift_vec[..., None, :]).astype(jnp.bfloat16)


def sigma_level(step_value):
    remaining = 1.0 - step_value / STEPS
    return flow_shift * remaining / (1.0 + (flow_shift - 1.0) * remaining)


def local(
    img_hidden,
    txt_hidden,
    img_mod,
    txt_mod,
    w_img_qkv,
    w_txt_qkv,
    w_out,
    w_head,
    text_lengths,
    latent,
    step,
):
    prompts = img_hidden.shape[1]
    img_rows = img_hidden.shape[2]
    txt_rows = txt_hidden.shape[2]
    dev_rows = img_rows + txt_rows
    model_width = img_hidden.shape[3]
    image_in = modulate(img_hidden[0], img_mod[0, :, 0], img_mod[0, :, 1])
    text_in = modulate(txt_hidden[0], txt_mod[0, :, 0], txt_mod[0, :, 1])
    full_img, full_txt, full_head = (
        lax.all_gather(w_img_qkv, ("guid", "req", "seq"), axis=0, tiled=True),
        lax.all_gather(w_txt_qkv, ("guid", "req", "seq"), axis=0, tiled=True),
        lax.all_gather(w_head, ("guid", "req", "seq"), axis=0, tiled=True),
    )
    attn_width = full_img.shape[1] // 3
    head_count = attn_width // HD
    qkv_image = jnp.einsum(
        "prd,de->pre", image_in, full_img, preferred_element_type=jnp.float32
    ).astype(jnp.bfloat16)
    qkv_text = jnp.einsum(
        "prd,de->pre", text_in, full_txt, preferred_element_type=jnp.float32
    ).astype(jnp.bfloat16)
    query_rows = qkv_image[..., :attn_width]
    key_rows = jnp.concatenate(
        [qkv_image[..., attn_width : 2 * attn_width], qkv_text[..., attn_width : 2 * attn_width]],
        axis=1,
    )
    value_rows = jnp.concatenate(
        [qkv_image[..., 2 * attn_width :], qkv_text[..., 2 * attn_width :]], axis=1
    )
    lengths = text_lengths[0]
    query_heads = query_rows.reshape(prompts, img_rows, head_count, HD)
    running = jnp.full((prompts, head_count, img_rows), -1e30, jnp.float32)
    key_piece = lax.all_gather(key_rows, "seq", axis=1, tiled=True)
    value_piece = lax.all_gather(value_rows, "seq", axis=1, tiled=True)
    piece_rows = key_piece.shape[1]
    key_heads = key_piece.reshape(prompts, piece_rows, head_count, HD)
    value_heads = value_piece.reshape(prompts, piece_rows, head_count, HD)
    scores = (
        jnp.einsum("pqhd,pkhd->phqk", query_heads, key_heads, preferred_element_type=jnp.float32)
        * 0.125
    )
    position = jnp.arange(piece_rows, dtype=jnp.int32)
    owner_dev = position // dev_rows
    offset = position % dev_rows
    text_pos = owner_dev * txt_rows + offset - img_rows
    allowed = (offset < img_rows)[None, :] | (text_pos[None, :] < lengths[:, None])
    scores = jnp.where(allowed[:, None, None, :], scores, -1e30)
    newest = jnp.maximum(running, jnp.max(scores, axis=-1))
    weights = jnp.exp(scores - newest[..., None])
    totals = jnp.sum(weights, axis=-1)
    accumulated = jnp.einsum(
        "phqk,pkhd->phqd",
        weights.astype(jnp.bfloat16),
        value_heads,
        preferred_element_type=jnp.float32,
    )
    running, totals, accumulated = (newest, totals, accumulated)
    mixture = accumulated / totals[..., None]
    attended = (
        jnp.transpose(mixture, (0, 2, 1, 3))
        .reshape(prompts, img_rows, attn_width)
        .astype(jnp.bfloat16)
    )
    flattened = attended.reshape(prompts * img_rows, attn_width)
    full_out = lax.all_gather(w_out, ("guid", "req", "seq"), axis=0, tiled=True)
    projected = jnp.dot(flattened, full_out, preferred_element_type=jnp.float32)
    residual = img_hidden[0].astype(jnp.float32) + img_mod[0, :, 2][:, None, :] * projected.reshape(
        prompts, img_rows, model_width
    )
    final_in = modulate(residual, img_mod[0, :, 3], img_mod[0, :, 4])
    guid_index = lax.axis_index("guid")
    half_width = latent.shape[2]
    own_start = guid_index * half_width
    other_start = (1 - guid_index) * half_width
    whole_velocity = jnp.einsum(
        "prd,dc->prc", final_in, full_head, preferred_element_type=jnp.float32
    )
    own_velocity = lax.dynamic_slice_in_dim(whole_velocity, own_start, half_width, 2)
    partner_part = lax.dynamic_slice_in_dim(whole_velocity, other_start, half_width, 2)
    other_velocity = partner(partner_part.astype(jnp.bfloat16), "guid", 0).astype(
        partner_part.dtype
    )
    cond_velocity = jnp.where(guid_index == 0, own_velocity, other_velocity)
    free_velocity = jnp.where(guid_index == 0, other_velocity, own_velocity)
    guided = free_velocity + guide_scale * (cond_velocity - free_velocity)
    step_value = step[0].astype(jnp.float32)
    advanced = latent + (sigma_level(step_value + 1.0) - sigma_level(step_value)) * guided
    return (advanced, guided)


def solution(mesh):
    placed = (
        P("guid", "req", "seq", None),
        P("guid", "req", "seq", None),
        P("guid", "req", None, None),
        P("guid", "req", None, None),
        P(("guid", "req", "seq"), None),
        P(("guid", "req", "seq"), None),
        P(("guid", "req", "seq"), None),
        P(("guid", "req", "seq"), None),
        P("guid", "req"),
        P("req", "seq", "guid"),
        P(),
    )
    return jax.shard_map(
        local,
        mesh=mesh,
        in_specs=placed,
        out_specs=(P("req", "seq", "guid"), P("req", "seq", "guid")),
        check_vma=False,
    )
```

profile of v0, /device:TPU:0, one launch (start us, length us, event | category | flops | bytes accessed | tf_op | source)
XLA Modules:
  0.0 542.6 jit_solution(7397176703256413804)
XLA Ops:
  8.7 1.1 convert_reduce_fusion.1
  9.8 1.2 fusion.38
  11.0 1.5 convert_reduce_fusion
  13.8 72.9 %all-gather.17.cloned.1.call-done = bf16[128,12,3072]{2,1,0:T(8,128)(2,1)} async-done(((bf16[1,12,3072]{2,1,0:T(8,128)(2,1)}), bf16[128,12,3072]{2,1,0:T(8,128)(2,1)}) %all-gather.17.cloned.1.call-update) | async-done | bytes 9437200 | tf_op jit(solution)/shard_map/all_gather | solution.py:54
  86.7 13.7 %reshape.191 = bf16[1536,3072,1]{1,0,2:T(8,128)(2,1)} reshape(bf16[128,12,3072]{2,1,0:T(8,128)(2,1)} %all-gather.17.cloned.1.call-done) | data formatting | bytes 18874368
  100.4 5.4 %convolution_convert_fusion.1 = bf16[6,12,3072]{2,1,0:T(8,128)(2,1)S(1)} fusion(bf16[1536,3072,1]{1,0,2:T(8,128)(2,1)} %reshape.191, bf16[1,6,12,1536]{3,2,1,0:T(8,128)(2,1)S(1)} %copy-done.1, f32[6,1536]{1,0:T(8,128)S(1)} %get-tuple-element.20, f32[6,1536]{1,0:T(8,128)S(1)} %get-tuple-element.21, f32[6,12]{1,0:T(8,128)S(1)} %add_rsqrt_fusion.1, ...), kind=kOutput, calls=%fused_computation.11 | convolution fusion | flops 680361984 | bytes 10175040 | tf_op jit(solution)/shard_map/prd,de->pre/dot_general | solution.py:62
  106.6 55.7 %all-gather.15.cloned.1.call-done = bf16[128,12,3072]{2,1,0:T(8,128)(2,1)} async-done(((bf16[1,12,3072]{2,1,0:T(8,128)(2,1)}), bf16[128,12,3072]{2,1,0:T(8,128)(2,1)}) %all-gather.15.cloned.1.call-update) | async-done | bytes 9437200 | tf_op jit(solution)/shard_map/all_gather | solution.py:53
  162.3 13.7 %reshape.190 = bf16[1536,3072,1]{1,0,2:T(8,128)(2,1)} reshape(bf16[128,12,3072]{2,1,0:T(8,128)(2,1)} %all-gather.15.cloned.1.call-done) | data formatting | bytes 18874368
  176.0 7.9 %convolution_convert_fusion = bf16[6,64,3072]{2,1,0:T(8,128)(2,1)S(1)} fusion(bf16[1536,3072,1]{1,0,2:T(8,128)(2,1)} %reshape.190, bf16[1,6,64,1536]{3,2,1,0:T(8,128)(2,1)S(1)} %copy-done, f32[6,1536]{1,0:T(8,128)S(1)} %get-tuple-element.25, f32[6,1536]{1,0:T(8,128)S(1)} %get-tuple-element.24, f32[6,64]{1,0:T(8,128)S(1)} %add_rsqrt_fusion.2, ...), kind=kOutput, calls=%fused_computation.10 | convolution fusion | flops 3628597248 | bytes 13052928 | tf_op jit(solution)/shard_map/prd,de->pre/dot_general | solution.py:59
  184.9 1.6 copy.34
  186.7 1.6 copy.31
  189.6 56.3 %all-gather.2 = bf16[128,12,64]{2,1,0:T(8,128)(2,1)S(1)} all-gather(bf16[1,12,64]{2,1,0:T(8,128)(2,1)S(1)} %bitcast.88), channel_id=1, replica_groups=mesh['guid'=2,'req'=4,'seq'=16] {'guid','req','seq'}, dimensions={0}, use_global_device_ids=true | all-gather | bytes 198144 | tf_op jit(solution)/shard_map/all_gather | solution.py:55
  248.6 68.5 %all-gather.11.cloned.1.call-done = bf16[6,1216,1024]{2,0,1:T(8,128)(2,1)} async-done(((bf16[6,76,1024]{2,0,1:T(8,128)(2,1)}), bf16[6,1216,1024]{2,0,1:T(8,128)(2,1)}) %all-gather.11.cloned.1.call-update) | async-done | bytes 14942224 | tf_op jit(solution)/shard_map/all_gather | solution.py:77
  317.1 27.3 %copy.35 = bf16[6,1216,1024]{1,2,0:T(8,128)(2,1)} copy(bf16[6,1216,1024]{2,0,1:T(8,128)(2,1)} %all-gather.11.cloned.1.call-done) | data formatting | bytes 29884416 | tf_op jit(solution)/shard_map/all_gather | solution.py:77
  344.4 100.9 %all-gather.9.cloned.1.call-done = bf16[6,1216,1024]{2,0,1:T(8,128)(2,1)} async-done(((bf16[6,76,1024]{2,0,1:T(8,128)(2,1)}), bf16[6,1216,1024]{2,0,1:T(8,128)(2,1)}) %all-gather.9.cloned.1.call-update) | async-done | bytes 14942224 | tf_op jit(solution)/shard_map/all_gather | solution.py:76
  445.3 26.9 %copy.32 = bf16[6,1216,1024]{1,2,0:T(8,128)(2,1)} copy(bf16[6,1216,1024]{2,0,1:T(8,128)(2,1)} %all-gather.9.cloned.1.call-done) | data formatting | bytes 29884416 | tf_op jit(solution)/shard_map/all_gather | solution.py:76
  472.2 15.9 %fusion = (f32[6,16,64]{2,1,0:T(8,128)S(1)}, f32[6,16,64,1216]{3,2,1,0:T(8,128)}) fusion(pred[6,1216]{1,0:T(8,128)(4,1)S(1)} %compare_or_fusion, bf16[6,1216,16,64]{1,3,2,0:T(8,128)(2,1)} %bitcast.82, bf16[6,64,16,64]{3,2,1,0:T(8,128)(2,1)S(1)} %reshape.170), kind=kOutput, calls=%fused_computation.2 | convolution fusion | flops 978708480 | bytes 45644928 | tf_op jit(solution)/shard_map/pqhd,pkhd->phqk/dot_general | solution.py:82
  488.0 14.0 %fusion.1 = f32[6,16,64]{2,1,0:T(8,128)S(1)} fusion(f32[6,16,64,1216]{3,2,1,0:T(8,128)} %get-tuple-element.17, f32[6,16,64]{2,1,0:T(8,128)S(1)} %broadcast_maximum_fusion, pred[6,1216]{1,0:T(8,128)(4,1)S(1)} %compare_or_fusion), kind=kLoop, calls=%fused_computation.3 | loop fusion | flops 29878272 | bytes 29940864 | tf_op jit(solution)/shard_map/reduce_sum | solution.py:93
  502.1 18.7 %fusion.11 = bf16[6,64,16,64]{3,1,2,0:T(8,128)(2,1)} fusion(bf16[6,1216,16,64]{1,3,2,0:T(8,128)(2,1)} %bitcast.83, f32[6,16,64,1216]{3,2,1,0:T(8,128)} %get-tuple-element.17, f32[6,16,64]{2,1,0:T(8,128)S(1)} %broadcast_maximum_fusion, pred[6,1216]{1,0:T(8,128)(4,1)S(1)} %compare_or_fusion, f32[6,64,16]{1,2,0:T(8,128)S(1)} %bitcast.87), kind=kOutput, calls=%fused_computation.15 | convolution fusion | flops 986972160 | bytes 45669504 | tf_op jit(solution)/shard_map/phqk,pkhd->phqd/dot_general | solution.py:94
  520.8 2.4 copy.36
  523.2 1.1 convert_element_type.60
  524.4 3.4 fusion.70
  529.6 3.0 collective-permute-start
  533.4 1.9 collective-permute-done
  (68 shorter events, 11.2 us)
Async XLA Ops:
  7.2 5.4 copy-start
  7.2 5.8 %copy-start.10 = (f32[1,6,2,1536]{3,2,1,0:T(2,128)S(1)}, f32[1,6,2,1536]{3,2,1,0:T(2,128)}, u32[]{:S(2)}) copy-start(f32[1,6,2,1536]{3,2,1,0:T(2,128)} %param.14) | copy-start | bytes 221188
  7.2 5.9 %copy-start.5 = (f32[1,6,5,1536]{3,0,2,1:T(1,128)S(1)}, f32[1,6,5,1536]{3,0,2,1:T(1,128)}, u32[]{:S(2)}) copy-start(f32[1,6,5,1536]{3,0,2,1:T(1,128)} %param.13) | copy-start | bytes 552964
  7.2 79.5 %all-gather.17.cloned.1.call-start = ((), (), s32[]{:S(2)}) async-start(), calls=%async_computation.4 | async-start | bytes 12681216 | tf_op jit(solution)/shard_map/all_gather | solution.py:54
  7.9 154.4 %all-gather.15.cloned.1.call-start = ((), (), s32[]{:S(2)}) async-start(), calls=%async_computation.3 | async-start | bytes 12681216 | tf_op jit(solution)/shard_map/all_gather | solution.py:53
  8.7 308.4 %all-gather.11.cloned.1.call-start = ((), (), s32[]{:S(2)}) async-start(), calls=%async_computation.1 | async-start | bytes 21168128 | tf_op jit(solution)/shard_map/all_gather | solution.py:77
  13.8 86.6 %copy-start.1 = (bf16[1,6,12,1536]{3,2,1,0:T(8,128)(2,1)S(1)}, bf16[1,6,12,1536]{3,2,1,0:T(8,128)(2,1)}, u32[]{:S(2)}) copy-start(bf16[1,6,12,1536]{3,2,1,0:T(8,128)(2,1)} %param.12) | copy-start | bytes 663556
  183.9 0.9 copy-start.3
  184.9 1.7 copy-start.2
  186.5 258.8 %all-gather.9.cloned.1.call-start = ((), (), s32[]{:S(2)}) async-start(), calls=%async_computation | async-start | bytes 21168128 | tf_op jit(solution)/shard_map/all_gather | solution.py:76
  186.6 2.4 copy-start.8
  186.6 3.0 copy-start.13
  186.7 60.1 %copy-start.6 = (f32[1,6,1,1536]{3,0,2,1:T(1,128)S(1)}, f32[1,6,1,1536]{3,0,2,1:T(1,128)}, u32[]{:S(2)}) copy-start(f32[1,6,1,1536]{3,0,2,1:T(1,128)} %get-tuple-element.9) | copy-start | bytes 110596
  186.7 60.1 %copy-start.7 = (f32[1,6,1,1536]{3,0,2,1:T(1,128)S(1)}, f32[1,6,1,1536]{3,0,2,1:T(1,128)}, u32[]{:S(2)}) copy-start(f32[1,6,1,1536]{3,0,2,1:T(1,128)} %get-tuple-element.12) | copy-start | bytes 110596
  186.7 60.8 %copy-start.14 = (s32[1,6]{1,0:T(1,128)S(1)}, s32[1,6]{1,0:T(1,128)}, u32[]{:S(2)}) copy-start(s32[1,6]{1,0:T(1,128)} %param.19) | copy-start | bytes 76
  188.3 336.0 %all-gather.13.cloned.1.call-start = ((), (), s32[]{:S(2)}) async-start(), calls=%async_computation.2 | async-start | bytes 3170304 | tf_op jit(solution)/shard_map/all_gather | solution.py:108
  527.7 1.0 copy-start.4
  527.7 1.0 copy-start.11
  527.8 1.0 copy-start.12
  527.8 7.5 %copy-start.9 = (f32[6,64,32]{1,2,0:T(8,128)S(1)}, f32[6,64,32]{1,2,0:T(8,128)}, u32[]{:S(2)}) copy-start(f32[6,64,32]{1,2,0:T(8,128)} %param.20) | copy-start | bytes 147460
  529.6 5.7 %collective-permute-start = (bf16[6,64,32]{1,2,0:T(8,128)(2,1)S(1)}, bf16[6,64,32]{1,2,0:T(8,128)(2,1)S(1)}, u32[]{:S(2)}, u32[]{:S(2)}) collective-permute-start(bf16[6,64,32]{1,2,0:T(8,128)(2,1)S(1)} %dynamic-slice_convert_fusion), channel_id=1, source_target_pairs={{0,64},{64,0},{1,65},{65,1},{2,66},{66,2},{3,67},{67,3},{4,68},{68... | collective-permute-start | bytes 73736 | tf_op jit(solution)/shard_map/ppermute | solution.py:16
Sparse Core Ops, SparseCore 0:
  11.1 75.5 all-gather.16
  89.7 72.5 all-gather.14
  186.6 130.4 all-gather.10
  319.1 126.1 all-gather.8
  448.2 65.3 all-gather.12
where the time goes:
time: 545 us; the launch traced here: 543 us
  waiting for transfers between devices  302 us (55%)
  local copies, waits for them, and re-layouts  93.9 us (17%)
  blocking collectives  56.3 us (10%)
  matrix products  52.2 us (10%)
  other arithmetic  20.3 us (4%)
  between operations  14.9 us (3%)
    all_gather x1, waiting for transfers between devices, local(): key_piece = lax.all_gather(key_rows, 'seq', axis=1, tiled=True)  101 us
    all_gather x1, waiting for transfers between devices, local(): lax.all_gather(w_txt_qkv, ('guid', 'req', 'seq'), axis=0, tiled=True)  72.9 us
    all_gather x1, waiting for transfers between devices, local(): value_piece = lax.all_gather(value_rows, 'seq', axis=1, tiled=True)  68.5 us
    all_gather x1, blocking collectives, local(): lax.all_gather(w_head, ('guid', 'req', 'seq'), axis=0, tiled=True)  56.3 us
    all_gather x1, waiting for transfers between devices, local(): lax.all_gather(w_img_qkv, ('guid', 'req', 'seq'), axis=0, tiled=True)  55.7 us
    unnamed x34, local copies, waits for them, and re-layouts  30.3 us
    all_gather x1, local copies, waits for them, and re-layouts, local(): value_piece = lax.all_gather(value_rows, 'seq', axis=1, tiled=True)  27.3 us
    all_gather x1, local copies, waits for them, and re-layouts, local(): key_piece = lax.all_gather(key_rows, 'seq', axis=1, tiled=True)  26.9 us
  transfers between devices with their start and end apart: 6, of which 5 were waited for; matrix products, arithmetic and copies ran while one was open for 25% of the time, Pallas kernels for 0%

commit v1 on v0

--- a/solution.py
+++ b/solution.py
@@ -8,6 +8,27 @@
 norm_epsilon = 1e-06
 flow_shift = 3.0
 guide_scale = 4.5
+
+
+def ring_gather(x, axis, dim):
+    size, index, width = (lax.axis_size(axis), lax.axis_index(axis), x.shape[dim])
+    right = [(i, (i + 1) % size) for i in range(size)]
+    backward = [(i, (i - 1) % size) for i in range(size)]
+    out = jnp.zeros((*x.shape[:dim], size * width, *x.shape[dim + 1 :]), x.dtype)
+    out = lax.dynamic_update_slice_in_dim(out, x, index * width, axis=dim)
+    from_left = from_right = x
+    middle = size // 2
+    for step in range(1, middle + 1):
+        from_left = lax.ppermute(from_left, axis, right)
+        out = lax.dynamic_update_slice_in_dim(
+            out, from_left, (index - step) % size * width, axis=dim
+        )
+        if step < size - middle:
+            from_right = lax.ppermute(from_right, axis, backward)
+            out = lax.dynamic_update_slice_in_dim(
+                out, from_right, (index + step) % size * width, axis=dim
+            )
+    return out
 
 
 def partner(value, axis, bit):
@@ -74,7 +95,7 @@
     query_heads = query_rows.reshape(prompts, img_rows, head_count, HD)
     running = jnp.full((prompts, head_count, img_rows), -1e30, jnp.float32)
     key_piece = lax.all_gather(key_rows, "seq", axis=1, tiled=True)
-    value_piece = lax.all_gather(value_rows, "seq", axis=1, tiled=True)
+    value_piece = ring_gather(value_rows, "seq", 1)
     piece_rows = key_piece.shape[1]
     key_heads = key_piece.reshape(prompts, piece_rows, head_count, HD)
     value_heads = value_piece.reshape(prompts, piece_rows, head_count, HD)

time: 545 us -> 940 us (1.72); the launches traced: 543 us -> 923 us
  local copies, waits for them, and re-layouts: 93.9 us -> 375 us
  waiting for transfers between devices: 302 us -> 354 us
  starting transfers between devices: 3.24 us -> 39.1 us
  blocking collectives: 56.3 us -> 67.7 us
    dynamic_update_slice x0 -> x16, local copies, waits for them, and re-layouts: none -> 273 us  [the longest x8 138 us: ring_gather(): lax.dynamic_update_slice_in_dim(out, from_left, (index - step) % size * w...]
    ppermute x0 -> x15, waiting for transfers between devices: none -> 221 us  [the longest x8 203 us: ring_gather(): from_left = lax.ppermute(from_left, axis, right)]
    all_gather x1, waiting for transfers between devices: 101 us -> 0.01 us  [local(): key_piece = lax.all_gather(key_rows, 'seq', axis=1, tiled=True)]
    all_gather x1 -> x0, waiting for transfers between devices: 68.5 us -> none  [local(): value_piece = lax.all_gather(value_rows, 'seq', axis=1, tiled=True)]
    ppermute x0 -> x15, starting transfers between devices: none -> 38.9 us  [the longest x7 37.7 us: ring_gather(): from_right = lax.ppermute(from_right, axis, backward)]
    ppermute x0 -> x15, local copies, waits for them, and re-layouts: none -> 27.3 us  [the longest x8 14.6 us: ring_gather(): from_left = lax.ppermute(from_left, axis, right)]
    all_gather x1 -> x0, local copies, waits for them, and re-layouts: 27.3 us -> none  [local(): value_piece = lax.all_gather(value_rows, 'seq', axis=1, tiled=True)]
    all_gather x1, waiting for transfers between devices: 72.9 us -> 52.9 us  [local(): lax.all_gather(w_txt_qkv, ('guid', 'req', 'seq'), axis=0, tiled=True)]
  transfers between devices with their start and end apart: 6 -> 20, of which waited for: 5 -> 14; matrix products, arithmetic and copies ran while one was open for 25% -> 45% of each run, Pallas kernels for 0% -> 0%
where the time goes in v1:
time: 940 us; the launch traced here: 923 us
  local copies, waits for them, and re-layouts  375 us (40%)
  waiting for transfers between devices  354 us (38%)
  blocking collectives  67.7 us (7%)
  matrix products  51.4 us (5%)
  starting transfers between devices  39.1 us (4%)
  other arithmetic  20.3 us (2%)
  between operations  15.2 us (2%)
    ppermute x8, waiting for transfers between devices, ring_gather(): from_left = lax.ppermute(from_left, axis, right)  203 us
    dynamic_update_slice x8, local copies, waits for them, and re-layouts, ring_gather(): lax.dynamic_update_slice_in_dim(out, from_left, (index - step) % size * w...  138 us
    dynamic_update_slice x7, local copies, waits for them, and re-layouts, ring_gather(): lax.dynamic_update_slice_in_dim(out, from_right, (index + step) % size *...  120 us
    all_gather x1, waiting for transfers between devices, local(): lax.all_gather(w_img_qkv, ('guid', 'req', 'seq'), axis=0, tiled=True)  73.5 us
    all_gather x1, blocking collectives, local(): lax.all_gather(w_head, ('guid', 'req', 'seq'), axis=0, tiled=True)  67.7 us
    all_gather x1, waiting for transfers between devices, local(): lax.all_gather(w_txt_qkv, ('guid', 'req', 'seq'), axis=0, tiled=True)  52.9 us
    ppermute x7, starting transfers between devices, ring_gather(): from_right = lax.ppermute(from_right, axis, backward)  37.7 us
    unnamed x48, local copies, waits for them, and re-layouts  31.5 us
  transfers between devices with their start and end apart: 20, of which 14 were waited for; matrix products, arithmetic and copies ran while one was open for 45% of the time, Pallas kernels for 0%

profile of v1, /device:TPU:0, one launch (start us, length us, event | category | flops | bytes accessed | tf_op | source)
XLA Modules:
  0.0 923.1 jit_solution(9650771829424685429)
XLA Ops:
  13.2 73.5 %all-gather.12.cloned.1.call-done = bf16[128,12,3072]{2,1,0:T(8,128)(2,1)} async-done(((bf16[1,12,3072]{2,1,0:T(8,128)(2,1)}), bf16[128,12,3072]{2,1,0:T(8,128)(2,1)}) %all-gather.12.cloned.1.call-update) | async-done | bytes 9437200 | tf_op jit(solution)/shard_map/all_gather | solution.py:74
  109.4 52.9 %all-gather.14.cloned.1.call-done = bf16[128,12,3072]{2,1,0:T(8,128)(2,1)} async-done(((bf16[1,12,3072]{2,1,0:T(8,128)(2,1)}), bf16[128,12,3072]{2,1,0:T(8,128)(2,1)}) %all-gather.14.cloned.1.call-update) | async-done | bytes 9437200 | tf_op jit(solution)/shard_map/all_gather | solution.py:75
  188.7 33.5 %collective-permute-done = bf16[6,76,1024]{2,1,0:T(8,128)(2,1)S(1)} collective-permute-done((bf16[6,76,1024]{2,1,0:T(8,128)(2,1)S(1)}, bf16[6,76,1024]{2,1,0:T(8,128)(2,1)S(1)}, u32[]{:S(2)}, u32[]{:S(2)}) %collective-permute-start) | collective-permute-done | bytes 933920 | tf_op jit(solution)/shard_map/ppermute | solution.py:22
  233.4 18.3 %collective-permute-done.2 = bf16[6,76,1024]{2,1,0:T(8,128)(2,1)S(1)} collective-permute-done((bf16[6,76,1024]{2,1,0:T(8,128)(2,1)S(1)}, bf16[6,76,1024]{2,1,0:T(8,128)(2,1)S(1)}, u32[]{:S(2)}, u32[]{:S(2)}) %collective-permute-start.2) | collective-permute-done | bytes 933920 | tf_op jit(solution)/shard_map/ppermute | solution.py:22
  257.4 36.6 %collective-permute-done.4 = bf16[6,76,1024]{2,1,0:T(8,128)(2,1)S(1)} collective-permute-done((bf16[6,76,1024]{2,1,0:T(8,128)(2,1)S(1)}, bf16[6,76,1024]{2,1,0:T(8,128)(2,1)S(1)}, u32[]{:S(2)}, u32[]{:S(2)}) %collective-permute-start.4) | collective-permute-done | bytes 933920 | tf_op jit(solution)/shard_map/ppermute | solution.py:22
  304.4 36.6 %collective-permute-done.6 = bf16[6,76,1024]{2,1,0:T(8,128)(2,1)S(1)} collective-permute-done((bf16[6,76,1024]{2,1,0:T(8,128)(2,1)S(1)}, bf16[6,76,1024]{2,1,0:T(8,128)(2,1)S(1)}, u32[]{:S(2)}, u32[]{:S(2)}) %collective-permute-start.6) | collective-permute-done | bytes 933920 | tf_op jit(solution)/shard_map/ppermute | solution.py:22
  351.4 36.6 %collective-permute-done.8 = bf16[6,76,1024]{2,1,0:T(8,128)(2,1)S(1)} collective-permute-done((bf16[6,76,1024]{2,1,0:T(8,128)(2,1)S(1)}, bf16[6,76,1024]{2,1,0:T(8,128)(2,1)S(1)}, u32[]{:S(2)}, u32[]{:S(2)}) %collective-permute-start.8) | collective-permute-done | bytes 933920 | tf_op jit(solution)/shard_map/ppermute | solution.py:22
  398.5 22.6 %collective-permute-done.10 = bf16[6,76,1024]{2,1,0:T(8,128)(2,1)S(1)} collective-permute-done((bf16[6,76,1024]{2,1,0:T(8,128)(2,1)S(1)}, bf16[6,76,1024]{2,1,0:T(8,128)(2,1)S(1)}, u32[]{:S(2)}, u32[]{:S(2)}) %collective-permute-start.10) | collective-permute-done | bytes 933920 | tf_op jit(solution)/shard_map/ppermute | solution.py:22
  426.5 19.2 %collective-permute-done.12 = bf16[6,76,1024]{2,1,0:T(8,128)(2,1)} collective-permute-done((bf16[6,76,1024]{2,1,0:T(8,128)(2,1)S(1)}, bf16[6,76,1024]{2,1,0:T(8,128)(2,1)}, u32[]{:S(2)}, u32[]{:S(2)}) %collective-permute-start.12) | collective-permute-done | bytes 933920 | tf_op jit(solution)/shard_map/ppermute | solution.py:22
  445.7 67.7 %all-gather.2 = bf16[128,12,64]{2,1,0:T(8,128)(2,1)S(1)} all-gather(bf16[1,12,64]{2,1,0:T(8,128)(2,1)S(1)} %bitcast.88), channel_id=1, replica_groups=mesh['guid'=2,'req'=4,'seq'=16] {'guid','req','seq'}, dimensions={0}, use_global_device_ids=true | all-gather | bytes 198144 | tf_op jit(solution)/shard_map/all_gather | solution.py:76
  542.3 17.2 %dynamic_update_slice.49 = bf16[6,1216,1024]{1,2,0:T(8,128)(2,1)} dynamic-update-slice(bf16[6,1216,1024]{1,2,0:T(8,128)(2,1)} %dynamic_update_slice.48, bf16[6,76,1024]{1,2,0:T(8,128)(2,1)S(1)} %copy.65, s32[]{:T(128)} %constant.152.clone.1, s32[]{:T(128)S(6)} %select_n.163, s32[]{:T(128)} %constant.152.clone.1) | dynamic-update-slice | bytes 1867780 | tf_op jit(solution)/shard_map/dynamic_update_slice | solution.py:23
  580.3 17.2 %dynamic_update_slice.51 = bf16[6,1216,1024]{1,2,0:T(8,128)(2,1)} dynamic-update-slice(bf16[6,1216,1024]{1,2,0:T(8,128)(2,1)} %dynamic_update_slice.50, bf16[6,76,1024]{1,2,0:T(8,128)(2,1)S(1)} %copy.67, s32[]{:T(128)} %constant.152.clone.1, s32[]{:T(128)S(6)} %select_n.167, s32[]{:T(128)} %constant.152.clone.1) | dynamic-update-slice | bytes 1867780 | tf_op jit(solution)/shard_map/dynamic_update_slice | solution.py:23
  599.4 17.2 %dynamic_update_slice.52 = bf16[6,1216,1024]{1,2,0:T(8,128)(2,1)} dynamic-update-slice(bf16[6,1216,1024]{1,2,0:T(8,128)(2,1)} %dynamic_update_slice.51, bf16[6,76,1024]{1,2,0:T(8,128)(2,1)S(1)} %copy.68, s32[]{:T(128)} %constant.152.clone.1, s32[]{:T(128)S(6)} %select_n.169, s32[]{:T(128)} %constant.152.clone.1) | dynamic-update-slice | bytes 1867780 | tf_op jit(solution)/shard_map/dynamic_update_slice | solution.py:28
  618.4 17.2 %dynamic_update_slice.53 = bf16[6,1216,1024]{1,2,0:T(8,128)(2,1)} dynamic-update-slice(bf16[6,1216,1024]{1,2,0:T(8,128)(2,1)} %dynamic_update_slice.52, bf16[6,76,1024]{1,2,0:T(8,128)(2,1)S(1)} %copy.69, s32[]{:T(128)} %constant.152.clone.1, s32[]{:T(128)S(6)} %select_n.171, s32[]{:T(128)} %constant.152.clone.1) | dynamic-update-slice | bytes 1867780 | tf_op jit(solution)/shard_map/dynamic_update_slice | solution.py:23
  637.5 17.2 %dynamic_update_slice.54 = bf16[6,1216,1024]{1,2,0:T(8,128)(2,1)} dynamic-update-slice(bf16[6,1216,1024]{1,2,0:T(8,128)(2,1)} %dynamic_update_slice.53, bf16[6,76,1024]{1,2,0:T(8,128)(2,1)S(1)} %copy.70, s32[]{:T(128)} %constant.152.clone.1, s32[]{:T(128)S(6)} %select_n.173, s32[]{:T(128)} %constant.152.clone.1) | dynamic-update-slice | bytes 1867780 | tf_op jit(solution)/shard_map/dynamic_update_slice | solution.py:28
  656.5 17.2 %dynamic_update_slice.55 = bf16[6,1216,1024]{1,2,0:T(8,128)(2,1)} dynamic-update-slice(bf16[6,1216,1024]{1,2,0:T(8,128)(2,1)} %dynamic_update_slice.54, bf16[6,76,1024]{1,2,0:T(8,128)(2,1)S(1)} %copy.71, s32[]{:T(128)} %constant.152.clone.1, s32[]{:T(128)S(6)} %select_n.175, s32[]{:T(128)} %constant.152.clone.1) | dynamic-update-slice | bytes 1867780 | tf_op jit(solution)/shard_map/dynamic_update_slice | solution.py:23
  675.6 17.2 %dynamic_update_slice.56 = bf16[6,1216,1024]{1,2,0:T(8,128)(2,1)} dynamic-update-slice(bf16[6,1216,1024]{1,2,0:T(8,128)(2,1)} %dynamic_update_slice.55, bf16[6,76,1024]{1,2,0:T(8,128)(2,1)S(1)} %copy.72, s32[]{:T(128)} %constant.152.clone.1, s32[]{:T(128)S(6)} %select_n.177, s32[]{:T(128)} %constant.152.clone.1) | dynamic-update-slice | bytes 1867780 | tf_op jit(solution)/shard_map/dynamic_update_slice | solution.py:28
  694.6 17.2 %dynamic_update_slice.57 = bf16[6,1216,1024]{1,2,0:T(8,128)(2,1)} dynamic-update-slice(bf16[6,1216,1024]{1,2,0:T(8,128)(2,1)} %dynamic_update_slice.56, bf16[6,76,1024]{1,2,0:T(8,128)(2,1)S(1)} %copy.73, s32[]{:T(128)} %constant.152.clone.1, s32[]{:T(128)S(6)} %select_n.179, s32[]{:T(128)} %constant.152.clone.1) | dynamic-update-slice | bytes 1867780 | tf_op jit(solution)/shard_map/dynamic_update_slice | solution.py:23
  713.6 17.2 %dynamic_update_slice.58 = bf16[6,1216,1024]{1,2,0:T(8,128)(2,1)} dynamic-update-slice(bf16[6,1216,1024]{1,2,0:T(8,128)(2,1)} %dynamic_update_slice.57, bf16[6,76,1024]{1,2,0:T(8,128)(2,1)S(1)} %copy.74, s32[]{:T(128)} %constant.152.clone.1, s32[]{:T(128)S(6)} %select_n.181, s32[]{:T(128)} %constant.152.clone.1) | dynamic-update-slice | bytes 1867780 | tf_op jit(solution)/shard_map/dynamic_update_slice | solution.py:28
  732.6 17.2 %dynamic_update_slice.59 = bf16[6,1216,1024]{1,2,0:T(8,128)(2,1)} dynamic-update-slice(bf16[6,1216,1024]{1,2,0:T(8,128)(2,1)} %dynamic_update_slice.58, bf16[6,76,1024]{1,2,0:T(8,128)(2,1)S(1)} %copy.75, s32[]{:T(128)} %constant.152.clone.1, s32[]{:T(128)S(6)} %select_n.183, s32[]{:T(128)} %constant.152.clone.1) | dynamic-update-slice | bytes 1867780 | tf_op jit(solution)/shard_map/dynamic_update_slice | solution.py:23
  751.6 17.4 %dynamic_update_slice.60 = bf16[6,1216,1024]{1,2,0:T(8,128)(2,1)} dynamic-update-slice(bf16[6,1216,1024]{1,2,0:T(8,128)(2,1)} %dynamic_update_slice.59, bf16[6,76,1024]{1,2,0:T(8,128)(2,1)S(1)} %copy.76, s32[]{:T(128)} %constant.152.clone.1, s32[]{:T(128)S(6)} %select_n.185, s32[]{:T(128)} %constant.152.clone.1) | dynamic-update-slice | bytes 1867780 | tf_op jit(solution)/shard_map/dynamic_update_slice | solution.py:28
  770.8 17.2 %dynamic_update_slice.61 = bf16[6,1216,1024]{1,2,0:T(8,128)(2,1)} dynamic-update-slice(bf16[6,1216,1024]{1,2,0:T(8,128)(2,1)} %dynamic_update_slice.60, bf16[6,76,1024]{1,2,0:T(8,128)(2,1)S(1)} %copy.77, s32[]{:T(128)} %constant.152.clone.1, s32[]{:T(128)S(6)} %select_n.187, s32[]{:T(128)} %constant.152.clone.1) | dynamic-update-slice | bytes 1867780 | tf_op jit(solution)/shard_map/dynamic_update_slice | solution.py:23
  826.0 26.9 %copy.62 = bf16[6,1216,1024]{1,2,0:T(8,128)(2,1)} copy(bf16[6,1216,1024]{2,0,1:T(8,128)(2,1)} %all-gather.8.cloned.1.call-done) | data formatting | bytes 29884416 | tf_op jit(solution)/shard_map/all_gather | solution.py:97
  882.8 18.0 %fusion.11 = bf16[6,64,16,64]{3,1,2,0:T(8,128)(2,1)} fusion(bf16[6,1216,16,64]{1,3,2,0:T(8,128)(2,1)} %bitcast.83, f32[6,16,64,1216]{3,2,1,0:T(8,128)} %get-tuple-element.17, f32[6,16,64]{2,1,0:T(8,128)S(1)} %broadcast_maximum_fusion, pred[6,1216]{1,0:T(8,128)(4,1)S(1)} %compare_or_fusion, f32[6,64,16]{1,2,0:T(8,128)S(1)} %bitcast.87), kind=kOutput, calls=%fused_computation.15 | convolution fusion | flops 986972160 | bytes 45669504 | tf_op jit(solution)/shard_map/phqk,pkhd->phqd/dot_general | solution.py:115
  (140 shorter events, 258.8 us)
Async XLA Ops:
  7.2 79.5 %all-gather.12.cloned.1.call-start = ((), (), s32[]{:S(2)}) async-start(), calls=%async_computation.2 | async-start | bytes 12681216 | tf_op jit(solution)/shard_map/all_gather | solution.py:74
  7.9 154.4 %all-gather.14.cloned.1.call-start = ((), (), s32[]{:S(2)}) async-start(), calls=%async_computation.3 | async-start | bytes 12681216 | tf_op jit(solution)/shard_map/all_gather | solution.py:75
  8.7 817.3 %all-gather.8.cloned.1.call-start = ((), (), s32[]{:S(2)}) async-start(), calls=%async_computation | async-start | bytes 21168128 | tf_op jit(solution)/shard_map/all_gather | solution.py:97
  181.5 264.2 %copy-start.20 = (bf16[12,64]{1,0:T(8,128)(2,1)S(1)}, bf16[12,64]{1,0:T(8,128)(2,1)}, u32[]{:S(2)}) copy-start(bf16[12,64]{1,0:T(8,128)(2,1)} %param.18) | copy-start | bytes 4612
  183.1 331.9 %copy-start.21 = (s32[1,6]{1,0:T(1,128)S(1)}, s32[1,6]{1,0:T(1,128)}, u32[]{:S(2)}) copy-start(s32[1,6]{1,0:T(1,128)} %param.19) | copy-start | bytes 76
  183.2 721.5 %all-gather.10.cloned.1.call-start = ((), (), s32[]{:S(2)}) async-start(), calls=%async_computation.1 | async-start | bytes 3170304 | tf_op jit(solution)/shard_map/all_gather | solution.py:129
  183.3 38.9 %collective-permute-start = (bf16[6,76,1024]{2,1,0:T(8,128)(2,1)S(1)}, bf16[6,76,1024]{2,1,0:T(8,128)(2,1)S(1)}, u32[]{:S(2)}, u32[]{:S(2)}) collective-permute-start(bf16[6,76,1024]{2,1,0:T(8,128)(2,1)S(1)} %pad_maximum_fusion.1), channel_id=1, source_target_pairs={{0,1},{1,2},{2,3},{3,4},{4,5},{5,6},{6,7},{7,8},{8,9},{9,10},{10,1... | collective-permute-start | bytes 2801672 | tf_op jit(solution)/shard_map/ppermute | solution.py:22
  184.5 42.1 %collective-permute-start.1 = (bf16[6,76,1024]{2,1,0:T(8,128)(2,1)S(1)}, bf16[6,76,1024]{2,1,0:T(8,128)(2,1)S(1)}, u32[]{:S(2)}, u32[]{:S(2)}) collective-permute-start(bf16[6,76,1024]{2,1,0:T(8,128)(2,1)S(1)} %pad_maximum_fusion.1), channel_id=1, source_target_pairs={{0,15},{1,0},{2,1},{3,2},{4,3},{5,4},{6,5},{7,6},{8,7},{9,8},{10,9... | collective-permute-start | bytes 2801672 | tf_op jit(solution)/shard_map/ppermute | solution.py:27
  222.2 71.8 %copy-start.5 = (bf16[6,76,1024]{2,1,0:T(8,128)(2,1)}, bf16[6,76,1024]{2,1,0:T(8,128)(2,1)S(1)}, u32[]{:S(2)}) copy-start(bf16[6,76,1024]{2,1,0:T(8,128)(2,1)S(1)} %collective-permute-done) | copy-start | bytes 2801668
  222.2 29.4 %collective-permute-start.2 = (bf16[6,76,1024]{2,1,0:T(8,128)(2,1)S(1)}, bf16[6,76,1024]{2,1,0:T(8,128)(2,1)S(1)}, u32[]{:S(2)}, u32[]{:S(2)}) collective-permute-start(bf16[6,76,1024]{2,1,0:T(8,128)(2,1)S(1)} %collective-permute-done), channel_id=1, source_target_pairs={{0,1},{1,2},{2,3},{3,4},{4,5},{5,6},{6,7},{7,8},{8,9},{9,10},{10,1... | collective-permute-start | bytes 2801672 | tf_op jit(solution)/shard_map/ppermute | solution.py:22
  227.6 24.1 %collective-permute-start.3 = (bf16[6,76,1024]{2,1,0:T(8,128)(2,1)S(1)}, bf16[6,76,1024]{2,1,0:T(8,128)(2,1)S(1)}, u32[]{:S(2)}, u32[]{:S(2)}) collective-permute-start(bf16[6,76,1024]{2,1,0:T(8,128)(2,1)S(1)} %collective-permute-done.1), channel_id=1, source_target_pairs={{0,15},{1,0},{2,1},{3,2},{4,3},{5,4},{6,5},{7,6},{8,7},{9,8},{10,9... | collective-permute-start | bytes 2801672 | tf_op jit(solution)/shard_map/ppermute | solution.py:27
  251.7 42.4 %collective-permute-start.4 = (bf16[6,76,1024]{2,1,0:T(8,128)(2,1)S(1)}, bf16[6,76,1024]{2,1,0:T(8,128)(2,1)S(1)}, u32[]{:S(2)}, u32[]{:S(2)}) collective-permute-start(bf16[6,76,1024]{2,1,0:T(8,128)(2,1)S(1)} %collective-permute-done.2), channel_id=1, source_target_pairs={{0,1},{1,2},{2,3},{3,4},{4,5},{5,6},{6,7},{7,8},{8,9},{9,10},{10,1... | collective-permute-start | bytes 2801672 | tf_op jit(solution)/shard_map/ppermute | solution.py:22
  252.6 46.0 %collective-permute-start.5 = (bf16[6,76,1024]{2,1,0:T(8,128)(2,1)S(1)}, bf16[6,76,1024]{2,1,0:T(8,128)(2,1)S(1)}, u32[]{:S(2)}, u32[]{:S(2)}) collective-permute-start(bf16[6,76,1024]{2,1,0:T(8,128)(2,1)S(1)} %collective-permute-done.3), channel_id=1, source_target_pairs={{0,15},{1,0},{2,1},{3,2},{4,3},{5,4},{6,5},{7,6},{8,7},{9,8},{10,9... | collective-permute-start | bytes 2801672 | tf_op jit(solution)/shard_map/ppermute | solution.py:27
  294.1 47.0 %collective-permute-start.6 = (bf16[6,76,1024]{2,1,0:T(8,128)(2,1)S(1)}, bf16[6,76,1024]{2,1,0:T(8,128)(2,1)S(1)}, u32[]{:S(2)}, u32[]{:S(2)}) collective-permute-start(bf16[6,76,1024]{2,1,0:T(8,128)(2,1)S(1)} %collective-permute-done.4), channel_id=1, source_target_pairs={{0,1},{1,2},{2,3},{3,4},{4,5},{5,6},{6,7},{7,8},{8,9},{9,10},{10,1... | collective-permute-start | bytes 2801672 | tf_op jit(solution)/shard_map/ppermute | solution.py:22
  298.6 47.0 %collective-permute-start.7 = (bf16[6,76,1024]{2,1,0:T(8,128)(2,1)S(1)}, bf16[6,76,1024]{2,1,0:T(8,128)(2,1)S(1)}, u32[]{:S(2)}, u32[]{:S(2)}) collective-permute-start(bf16[6,76,1024]{2,1,0:T(8,128)(2,1)S(1)} %collective-permute-done.5), channel_id=1, source_target_pairs={{0,15},{1,0},{2,1},{3,2},{4,3},{5,4},{6,5},{7,6},{8,7},{9,8},{10,9... | collective-permute-start | bytes 2801672 | tf_op jit(solution)/shard_map/ppermute | solution.py:27
  341.1 47.0 %collective-permute-start.8 = (bf16[6,76,1024]{2,1,0:T(8,128)(2,1)S(1)}, bf16[6,76,1024]{2,1,0:T(8,128)(2,1)S(1)}, u32[]{:S(2)}, u32[]{:S(2)}) collective-permute-start(bf16[6,76,1024]{2,1,0:T(8,128)(2,1)S(1)} %collective-permute-done.6), channel_id=1, source_target_pairs={{0,1},{1,2},{2,3},{3,4},{4,5},{5,6},{6,7},{7,8},{8,9},{9,10},{10,1... | collective-permute-start | bytes 2801672 | tf_op jit(solution)/shard_map/ppermute | solution.py:22
  345.6 47.0 %collective-permute-start.9 = (bf16[6,76,1024]{2,1,0:T(8,128)(2,1)S(1)}, bf16[6,76,1024]{2,1,0:T(8,128)(2,1)S(1)}, u32[]{:S(2)}, u32[]{:S(2)}) collective-permute-start(bf16[6,76,1024]{2,1,0:T(8,128)(2,1)S(1)} %collective-permute-done.7), channel_id=1, source_target_pairs={{0,15},{1,0},{2,1},{3,2},{4,3},{5,4},{6,5},{7,6},{8,7},{9,8},{10,9... | collective-permute-start | bytes 2801672 | tf_op jit(solution)/shard_map/ppermute | solution.py:27
  388.1 33.0 %collective-permute-start.10 = (bf16[6,76,1024]{2,1,0:T(8,128)(2,1)S(1)}, bf16[6,76,1024]{2,1,0:T(8,128)(2,1)S(1)}, u32[]{:S(2)}, u32[]{:S(2)}) collective-permute-start(bf16[6,76,1024]{2,1,0:T(8,128)(2,1)S(1)} %collective-permute-done.8), channel_id=1, source_target_pairs={{0,1},{1,2},{2,3},{3,4},{4,5},{5,6},{6,7},{7,8},{8,9},{9,10},{10,1... | collective-permute-start | bytes 2801672 | tf_op jit(solution)/shard_map/ppermute | solution.py:22
  392.6 28.5 %collective-permute-start.11 = (bf16[6,76,1024]{2,1,0:T(8,128)(2,1)S(1)}, bf16[6,76,1024]{2,1,0:T(8,128)(2,1)}, u32[]{:S(2)}, u32[]{:S(2)}) collective-permute-start(bf16[6,76,1024]{2,1,0:T(8,128)(2,1)S(1)} %collective-permute-done.9), channel_id=1, source_target_pairs={{0,15},{1,0},{2,1},{3,2},{4,3},{5,4},{6,5},{7,6},{8,7},{9,8},{10,9... | collective-permute-start | bytes 2801672 | tf_op jit(solution)/shard_map/ppermute | solution.py:27
  421.0 94.0 %copy-start.13 = (bf16[6,76,1024]{2,1,0:T(8,128)(2,1)}, bf16[6,76,1024]{2,1,0:T(8,128)(2,1)S(1)}, u32[]{:S(2)}) copy-start(bf16[6,76,1024]{2,1,0:T(8,128)(2,1)S(1)} %collective-permute-done.10) | copy-start | bytes 2801668
  421.1 24.7 %collective-permute-start.12 = (bf16[6,76,1024]{2,1,0:T(8,128)(2,1)S(1)}, bf16[6,76,1024]{2,1,0:T(8,128)(2,1)}, u32[]{:S(2)}, u32[]{:S(2)}) collective-permute-start(bf16[6,76,1024]{2,1,0:T(8,128)(2,1)S(1)} %collective-permute-done.10), channel_id=1, source_target_pairs={{0,1},{1,2},{2,3},{3,4},{4,5},{5,6},{6,7},{7,8},{8,9},{9,10},{10,1... | collective-permute-start | bytes 2801672 | tf_op jit(solution)/shard_map/ppermute | solution.py:22
  421.1 366.9 %collective-permute-start.13 = (bf16[6,76,1024]{2,1,0:T(8,128)(2,1)}, bf16[6,76,1024]{2,1,0:T(8,128)(2,1)}, u32[]{:S(2)}, u32[]{:S(2)}) collective-permute-start(bf16[6,76,1024]{2,1,0:T(8,128)(2,1)} %collective-permute-done.11), channel_id=1, source_target_pairs={{0,15},{1,0},{2,1},{3,2},{4,3},{5,4},{6,5},{7,6},{8,7},{9,8},{10,9... | collective-permute-start | bytes 2801672 | tf_op jit(solution)/shard_map/ppermute | solution.py:27
  445.7 361.3 %collective-permute-start.14 = (bf16[6,76,1024]{2,1,0:T(8,128)(2,1)}, bf16[6,76,1024]{2,1,0:T(8,128)(2,1)}, u32[]{:S(2)}, u32[]{:S(2)}) collective-permute-start(bf16[6,76,1024]{2,1,0:T(8,128)(2,1)} %collective-permute-done.12), channel_id=1, source_target_pairs={{0,1},{1,2},{2,3},{3,4},{4,5},{5,6},{6,7},{7,8},{8,9},{9,10},{10,1... | collective-permute-start | bytes 2801672 | tf_op jit(solution)/shard_map/ppermute | solution.py:22
  910.0 5.7 collective-permute-start.15
  (18 other events, 293.1 us)
Sparse Core Ops, SparseCore 0:
  11.1 75.5 all-gather.11
  89.7 72.5 all-gather.13
  183.3 227.5 all-gather.7
  421.2 81.6 all-gather.9
